TPU v7x, 32 devices: a whole 2x2x4 slice. The times are simulated.
32 devices in a mesh: freq: 4 (over y, core), row: 8 (over z, x).
Axes of the slice: x: 2, y: 2, z: 4, core: 2. Of those that a mesh axis runs over, the one named last changes fastest.
Arguments:
- traces: bfloat16 [2, 8192, 8192], P(None, ('freq', 'row')), may hold values from -1.1953125 to 1.1953125
- prior: bfloat16 [4, 2, 8192, 8192], P('freq', None, None, 'row'), may hold values from -0.796875 to 0.796875
- bins: int32 [4], replicated, may hold values from 64 to 255
- panels: int32 [2], replicated, may hold values from 0 to 31
Outputs:
- multiples: bfloat16 [4, 2, 8192, 8192], P('freq', None, 'row')
- spectrum: bfloat16 [4, 2, 8192, 8192], P('freq', None, None, 'row')
All inputs are finite; a program needn't handle non-finite values.
Results may differ from a plain program's by a relative error of at most 0.0077.
Values may be sent and summed in bfloat16 or wider, within the bound.
No kernel may reach another device: no remote copies, remote signals or barrier semaphores. Data moves between devices by JAX's collectives and lax.ppermute only.
A program may use at most 640 MiB of HBM per device.

v0:
```python
import math
import jax
import jax.numpy as jnp
from jax import lax
from jax.sharding import PartitionSpec as P

NT_REC = 1024
PANEL = 256
STEPS = 2
BLOCK_START = 1022


def spread(value, axis, source):
    kept = jnp.where(lax.axis_index(axis) == source, value, 0).astype(value.dtype)
    return lax.psum(kept, axis)


def complex_terms(left, right):
    dims = (((0,), (1,)), ((), ()))

    def product(first, second):
        return lax.dot_general(first, second, dims, preferred_element_type=jnp.float32)

    real_part = product(left[0], right[0]) - product(left[1], right[1])
    imag_part = product(left[0], right[1]) + product(left[1], right[0])
    return (real_part, imag_part)


def body(traces, prior, bins, panels):
    sample_count, shots_local, receivers = traces.shape
    row_count = lax.axis_size("row")
    block_rows = receivers // row_count
    sample_index = BLOCK_START + jnp.arange(sample_count, dtype=jnp.int32)
    turn_count = bins[:, None] * sample_index[None, :] % NT_REC
    angles = 2.0 * math.pi / NT_REC * turn_count.astype(jnp.float32)
    twiddle = jnp.stack([jnp.cos(angles), -jnp.sin(angles)], axis=1).astype(jnp.bfloat16)
    own_twiddle = lax.dynamic_index_in_dim(twiddle, lax.axis_index("freq"), 0, keepdims=False)
    by_row = lax.all_to_all(traces, "row", split_axis=2, concat_axis=1, tiled=True)
    gathered = lax.all_gather(by_row, "freq", axis=1, tiled=True)
    transformed = jnp.einsum(
        "tsb,ct->csb", gathered, own_twiddle, preferred_element_type=jnp.float32
    ).astype(jnp.bfloat16)
    spectrum = (prior[0].astype(jnp.float32) + transformed.astype(jnp.float32)).astype(jnp.bfloat16)
    panels_each = block_rows // PANEL
    real_sum = jnp.zeros((block_rows, receivers), jnp.float32)
    imag_sum = jnp.zeros((block_rows, receivers), jnp.float32)
    for panel_step in range(STEPS):
        chosen = panels[panel_step]
        owner = chosen // panels_each
        offset = chosen % panels_each * PANEL
        own_rows = lax.dynamic_slice_in_dim(spectrum, offset, PANEL, 2)
        panel_data = spread(own_rows, "row", owner)
        left = lax.dynamic_slice_in_dim(spectrum, chosen * PANEL, PANEL, 1)
        real_part, imag_part = complex_terms(left, panel_data)
        real_sum = real_sum + real_part
        imag_sum = imag_sum + imag_part
    return (jnp.stack([real_sum, imag_sum])[None].astype(jnp.bfloat16), spectrum[None])


def solution(mesh):
    return jax.shard_map(
        body,
        mesh=mesh,
        in_specs=(P(None, ("freq", "row"), None), P("freq", None, None, "row"), P(), P()),
        out_specs=(P("freq", None, "row", None), P("freq", None, None, "row")),
        check_vma=False,
    )
```

profile of v0, /device:TPU:0, one launch (start us, length us, event | category | flops | bytes accessed | tf_op | source)
XLA Modules:
  0.0 1370.1 jit_solution(301745803882222178)
XLA Ops:
  7.2 0.0 all-gather.2.cloned.1.call-start
  7.2 21.0 %copy.21 = bf16[2,256,8192]{1,0,2:T(2,128)(2,1)} copy(bf16[2,256,8192]{2,1,0:T(8,128)(2,1)} %param.4) | data formatting | bytes 16777216 | tf_op args[0]
  28.2 190.4 %all_to_all.18 = bf16[2,256,8192]{1,0,2:T(2,128)(2,1)} all-to-all(bf16[2,256,8192]{1,0,2:T(2,128)(2,1)} %copy.21), channel_id=1, replica_groups=mesh['freq'=4,'row'=8] {'row'}, dimensions={2} | all-to-all | bytes 16777216 | tf_op jit(solution)/shard_map/all_to_all | solution.py:38
  218.6 30.5 %copy.22 = bf16[2,8,256,1024]{3,0,2,1:T(2,128)(2,1)} copy(bf16[2,8,256,1024]{2,0,3,1:T(2,128)(2,1)} %bitcast.60) | data formatting | bytes 16777216 | tf_op jit(solution)/shard_map/all_to_all | solution.py:38
  249.1 0.0 copy-start.1
  249.1 0.0 copy-start.2
  249.1 0.0 all-gather.2.cloned.1.call-update
  249.1 0.0 all-reduce.3.cloned.1.call-start
  249.2 0.6 copy-done.1
  249.8 0.6 fusion.49
  255.3 0.0 copy-done.2
  255.3 0.1 cosine_convert_fusion
  255.4 0.2 fusion.45
  255.6 194.4 %all-gather.2.cloned.1.call-done = bf16[2,8192,1024]{2,0,1:T(2,128)(2,1)} async-done(((bf16[2,2048,1024]{2,0,1:T(2,128)(2,1)}), bf16[2,8192,1024]{2,0,1:T(2,128)(2,1)}) %all-gather.2.cloned.1.call-update) | async-done | bytes 33554448 | tf_op jit(solution)/shard_map/all_gather | solution.py:39
  449.9 145.3 %fusion = bf16[2,8192,1024]{2,0,1:T(2,128)(2,1)} fusion(bf16[1,2,8192,1024]{3,2,1,0:T(8,128)(2,1)} %param.5, bf16[2,8192,1024]{2,0,1:T(2,128)(2,1)} %all-gather.2.cloned.1.call-done, bf16[2,2]{1,0:T(2,128)(2,1)S(1)} %fusion.45), kind=kOutput, calls=%fused_computation.1 | convolution fusion | flops 150994944 | bytes 100663304 | tf_op jit(solution)/shard_map/tsb,ct->csb/dot_general | solution.py:40
  595.3 17.1 %broadcast_select_fusion.1 = (bf16[2,8192,256]{2,0,1:T(2,128)(2,1)}, bf16[2,8192,256]{2,0,1:T(2,128)(2,1)}) fusion(pred[]{:T(512)S(6)} %eq.11, bf16[2,8192,1024]{2,0,1:T(2,128)(2,1)} %fusion, s32[]{:T(128)S(6)} %select_n.71, s32[]{:T(128)S(6)} %select_n.77, pred[]{:T(512)S(6)} %eq.12), kind=kLoop, calls=%fused_computation.7 | loop fusion | flops 8388608 | bytes 33554440 | tf_op jit(solution)/shard_map/jit(_where)/select_n | solution.py:14
  612.3 0.0 all-reduce.3.cloned.1.call-update
  613.6 23.4 %copy.23 = bf16[1,2,8192,1024]{3,2,1,0:T(8,128)(2,1)} copy(bf16[1,2,8192,1024]{3,1,2,0:T(2,128)(2,1)} %bitcast.58) | data formatting | bytes 67108864
  637.0 6.3 constant_dynamic-slice_fusion.3
  643.3 479.6 %all-reduce.3.cloned.1.call-done = (bf16[2,8192,256]{2,0,1:T(2,128)(2,1)}, bf16[2,8192,256]{2,0,1:T(2,128)(2,1)}) async-done(((bf16[2,8192,256]{2,0,1:T(2,128)(2,1)}, bf16[2,8192,256]{2,0,1:T(2,128)(2,1)}), (bf16[2,8192,256]{2,0,1:T(2,128)(2,1)}, bf16[2,8192,256]{2,0,1:T(2,128)(2,1)})) %all-reduce.3.cloned.1.call-update) | async-done | bytes 16777232 | tf_op jit(solution)/shard_map/psum | solution.py:15
  1122.9 33.0 %fusion.47 = (bf16[1,8192,256]{2,0,1:T(2,128)(2,1)}, bf16[1,8192,256]{2,0,1:T(2,128)(2,1)}, bf16[1,8192,256]{2,0,1:T(2,128)(2,1)}, bf16[1,8192,256]{2,0,1:T(2,128)(2,1)}) fusion(bf16[2,8192,256]{2,0,1:T(2,128)(2,1)} %get-tuple-element.12, bf16[2,8192,256]{2,0,1:T(2,128)(2,1)} %get-tuple-element.13), kind=kLoop, calls=%fused_computation.67 | loop fusion | bytes 33554432 | tf_op jit(solution)/shard_map/slice | solution.py:24
  1155.9 0.0 copy-start
  1155.9 19.5 %fusion.11 = f32[1024,8192]{1,0:T(8,128)} fusion(bf16[1,8192,256]{2,0,1:T(2,128)(2,1)} %get-tuple-element.28, bf16[1,256,1024]{2,0,1:T(2,128)(2,1)} %get-tuple-element.17), kind=kOutput, calls=%fused_computation.18 | convolution fusion | flops 4294967296 | bytes 38273024 | tf_op jit(solution)/shard_map/dot_general | solution.py:22
  1175.3 0.0 copy-done
  1175.3 16.5 %fusion.13 = f32[1024,8192]{1,0:T(8,128)} fusion(bf16[1,8192,256]{2,0,1:T(2,128)(2,1)} %get-tuple-element.29, bf16[1,256,1024]{2,0,1:T(2,128)(2,1)S(1)} %copy-done), kind=kOutput, calls=%fused_computation.20 | convolution fusion | flops 4294967296 | bytes 38273024 | tf_op jit(solution)/shard_map/dot_general | solution.py:22
  1191.9 16.5 %fusion.15 = f32[1024,8192]{1,0:T(8,128)} fusion(bf16[1,8192,256]{2,0,1:T(2,128)(2,1)} %get-tuple-element.29, bf16[1,256,1024]{2,0,1:T(2,128)(2,1)S(1)} %get-tuple-element.16), kind=kOutput, calls=%fused_computation.22 | convolution fusion | flops 4294967296 | bytes 38273024 | tf_op jit(solution)/shard_map/dot_general | solution.py:22
  1208.4 16.5 %fusion.9 = f32[1024,8192]{1,0:T(8,128)} fusion(bf16[1,8192,256]{2,0,1:T(2,128)(2,1)} %get-tuple-element.28, bf16[1,256,1024]{2,0,1:T(2,128)(2,1)S(1)} %get-tuple-element.16), kind=kOutput, calls=%fused_computation.16 | convolution fusion | flops 4294967296 | bytes 38273024 | tf_op jit(solution)/shard_map/dot_general | solution.py:22
  1225.0 16.5 %fusion.7 = f32[1024,8192]{1,0:T(8,128)} fusion(bf16[1,8192,256]{2,0,1:T(2,128)(2,1)} %get-tuple-element.20, bf16[1,256,1024]{2,0,1:T(2,128)(2,1)S(1)} %get-tuple-element.15), kind=kOutput, calls=%fused_computation.14 | convolution fusion | flops 4294967296 | bytes 38273024 | tf_op jit(solution)/shard_map/dot_general | solution.py:22
  1241.5 17.5 %fusion.3 = f32[1024,8192]{1,0:T(8,128)} fusion(bf16[1,8192,256]{2,0,1:T(2,128)(2,1)} %get-tuple-element.21, bf16[1,256,1024]{2,0,1:T(2,128)(2,1)S(1)} %get-tuple-element.15), kind=kOutput, calls=%fused_computation.10 | convolution fusion | flops 4294967296 | bytes 38273024 | tf_op jit(solution)/shard_map/dot_general | solution.py:22
  1259.0 40.7 %fusion.1 = bf16[1,1,1024,8192]{3,2,1,0:T(8,128)(2,1)} fusion(f32[1024,8192]{1,0:T(8,128)} %fusion.7, f32[1024,8192]{1,0:T(8,128)} %fusion.15, f32[1024,8192]{1,0:T(8,128)} %fusion.11, bf16[1,8192,256]{2,0,1:T(2,128)(2,1)} %get-tuple-element.21, bf16[1,256,1024]{2,0,1:T(2,128)(2,1)S(1)} %get-tuple-element.14), kind=kOutput, calls=%fused_computation.8 | convolution fusion | flops 4328521728 | bytes 122159104 | tf_op jit(solution)/shard_map/dot_general | solution.py:22
  1299.7 40.6 %fusion.2 = bf16[1,1,1024,8192]{3,2,1,0:T(8,128)(2,1)} fusion(f32[1024,8192]{1,0:T(8,128)} %fusion.3, f32[1024,8192]{1,0:T(8,128)} %fusion.9, f32[1024,8192]{1,0:T(8,128)} %fusion.13, bf16[1,8192,256]{2,0,1:T(2,128)(2,1)} %get-tuple-element.20, bf16[1,256,1024]{2,0,1:T(2,128)(2,1)S(1)} %get-tuple-element.14), kind=kOutput, calls=%fused_computation.9 | convolution fusion | flops 4328521728 | bytes 122159104 | tf_op jit(solution)/shard_map/dot_general | solution.py:22
  1340.3 23.0 %pad_maximum_fusion = bf16[1,2,1024,8192]{3,2,1,0:T(8,128)(2,1)} fusion(bf16[1,1,1024,8192]{3,2,1,0:T(8,128)(2,1)} %fusion.2, bf16[1,1,1024,8192]{3,2,1,0:T(8,128)(2,1)} %fusion.1), kind=kLoop, calls=%fused_computation.3 | loop fusion | flops 16777216 | bytes 67108864 | tf_op jit(solution)/shard_map/stack | solution.py:57
  (1 shorter events, 0.0 us)
Async XLA Ops:
  7.2 442.8 %all-gather.2.cloned.1.call-start = ((), (), s32[]{:S(2)}) async-start(), calls=%async_computation.1 | async-start | bytes 41943040 | tf_op jit(solution)/shard_map/all_gather | solution.py:39
  249.1 0.7 copy-start.1
  249.1 6.2 copy-start.2
  249.1 873.8 %all-reduce.3.cloned.1.call-start = ((), (), s32[]{:S(2)}) async-start(), calls=%async_computation.2 | async-start | bytes 33554432 | tf_op jit(solution)/shard_map/psum | solution.py:15
  1155.9 19.5 %copy-start = (bf16[1,256,1024]{2,0,1:T(2,128)(2,1)S(1)}, bf16[1,256,1024]{2,0,1:T(2,128)(2,1)}, u32[]{:S(2)}) copy-start(bf16[1,256,1024]{2,0,1:T(2,128)(2,1)} %get-tuple-element.17) | copy-start | bytes 1572868
Sparse Core Ops, SparseCore 0:
  249.2 200.6 all-gather.1
  612.5 510.3 all-reduce.2
where the time goes:
time: 1370 us
  waiting for transfers between devices  674 us (49%)
  matrix products  330 us (24%)
  blocking collectives  190 us (14%)
  local copies, waits for them, and re-layouts  115 us (8%)
  other arithmetic  40.3 us (3%)
  between operations  20.2 us (1%)
    psum x1, waiting for transfers between devices, spread(): return lax.psum(kept, axis)  480 us
    all_gather x1, waiting for transfers between devices, body(): gathered = lax.all_gather(by_row, 'freq', axis=1, tiled=True)  194 us
    all_to_all x1, blocking collectives, body(): lax.all_to_all(traces, 'row', split_axis=2, concat_axis=1, tiled=True)  190 us
    dot_general x8, matrix products, product(): lax.dot_general(first, second, dims, preferred_element_type=jnp.float32)  184 us
    dot_general x1, matrix products, body(): jnp.einsum('tsb,ct->csb', gathered, own_twiddle, preferred_element_type=j...  145 us
    unnamed x8, local copies, waits for them, and re-layouts  45 us
    slice x2, local copies, waits for them, and re-layouts, complex_terms(): real_part = product(left[0], right[0]) - product(left[1], right[1])  39.3 us
    all_to_all x1, local copies, waits for them, and re-layouts, body(): lax.all_to_all(traces, 'row', split_axis=2, concat_axis=1, tiled=True)  30.5 us
  transfers between devices with their start and end apart: 2, of which 2 were waited for; matrix products, arithmetic and copies ran while one was open for 2% of the time, Pallas kernels for 0%

commit v1 on v0

--- a/solution.py
+++ b/solution.py
@@ -8,6 +8,23 @@
 PANEL = 256
 STEPS = 2
 BLOCK_START = 1022
+
+
+def joined_along(tiles, dim):
+    tiles = jnp.moveaxis(tiles, 0, dim)
+    shape = tiles.shape
+    return tiles.reshape(*shape[:dim], shape[dim] * shape[dim + 1], *shape[dim + 2 :])
+
+
+def grow_blocks(array, axis):
+    size, here = (lax.axis_size(axis), lax.axis_index(axis))
+    parts, bit = (array[None], 1)
+    while bit < size:
+        received = lax.ppermute(parts, axis, [(i, i ^ bit) for i in range(size)])
+        low = here & bit == 0
+        parts = jnp.concatenate([jnp.where(low, parts, received), jnp.where(low, received, parts)])
+        bit *= 2
+    return parts
 
 
 def spread(value, axis, source):
@@ -36,7 +53,7 @@
     twiddle = jnp.stack([jnp.cos(angles), -jnp.sin(angles)], axis=1).astype(jnp.bfloat16)
     own_twiddle = lax.dynamic_index_in_dim(twiddle, lax.axis_index("freq"), 0, keepdims=False)
     by_row = lax.all_to_all(traces, "row", split_axis=2, concat_axis=1, tiled=True)
-    gathered = lax.all_gather(by_row, "freq", axis=1, tiled=True)
+    gathered = joined_along(grow_blocks(by_row, "freq"), 1)
     transformed = jnp.einsum(
         "tsb,ct->csb", gathered, own_twiddle, preferred_element_type=jnp.float32
     ).astype(jnp.bfloat16)

time: 1370 us -> 1690 us (1.23)
  waiting for transfers between devices: 674 us -> 848 us
  other arithmetic: 40.3 us -> 174 us
    ppermute x0 -> x2, waiting for transfers between devices: none -> 369 us  [grow_blocks(): received = lax.ppermute(parts, axis, [(i, i ^ bit) for i in range(size)])]
    all_gather x1 -> x0, waiting for transfers between devices: 194 us -> none  [body(): gathered = lax.all_gather(by_row, 'freq', axis=1, tiled=True)]
    concatenate x0 -> x2, other arithmetic: none -> 74.1 us  [grow_blocks(): jnp.concatenate([jnp.where(low, parts, received), jnp.where(low, received...]
    select_n x0 -> x2, other arithmetic: none -> 58.8 us  [grow_blocks(): jnp.where(low, parts, received)]
    unnamed x8 -> x12, local copies, waits for them, and re-layouts: 45 us -> 44.5 us
  transfers between devices with their start and end apart: 2 -> 3, of which waited for: 2 -> 3; matrix products, arithmetic and copies ran while one was open for 2% -> 2% of each run, Pallas kernels for 0% -> 0%
where the time goes in v1:
time: 1690 us; the launch traced here: 1680 us
  waiting for transfers between devices  848 us (50%)
  matrix products  330 us (20%)
  blocking collectives  190 us (11%)
  other arithmetic  174 us (10%)
  local copies, waits for them, and re-layouts  115 us (7%)
  between operations  20.3 us (1%)
    psum x1, waiting for transfers between devices, spread(): return lax.psum(kept, axis)  479 us
    ppermute x2, waiting for transfers between devices, grow_blocks(): received = lax.ppermute(parts, axis, [(i, i ^ bit) for i in range(size)])  369 us
    all_to_all x1, blocking collectives, body(): lax.all_to_all(traces, 'row', split_axis=2, concat_axis=1, tiled=True)  190 us
    dot_general x8, matrix products, product(): lax.dot_general(first, second, dims, preferred_element_type=jnp.float32)  185 us
    dot_general x1, matrix products, body(): jnp.einsum('tsb,ct->csb', gathered, own_twiddle, preferred_element_type=j...  145 us
    concatenate x2, other arithmetic, grow_blocks(): jnp.concatenate([jnp.where(low, parts, received), jnp.where(low, received...  74.1 us
    select_n x2, other arithmetic, grow_blocks(): jnp.where(low, parts, received)  58.8 us
    unnamed x12, local copies, waits for them, and re-layouts  44.5 us
  transfers between devices with their start and end apart: 3, of which 3 were waited for; matrix products, arithmetic and copies ran while one was open for 2% of the time, Pallas kernels for 0%

profile of v1, /device:TPU:0, one launch (start us, length us, event | category | flops | bytes accessed | tf_op | source)
XLA Modules:
  0.0 1678.5 jit_solution(9323283265807699003)
XLA Ops:
  7.2 0.0 all-reduce.3.cloned.1.call-start
  7.2 21.0 %copy.21 = bf16[2,256,8192]{1,0,2:T(2,128)(2,1)} copy(bf16[2,256,8192]{2,1,0:T(8,128)(2,1)} %param.4) | data formatting | bytes 16777216 | tf_op args[0]
  28.2 190.4 %all_to_all.15 = bf16[2,256,8192]{1,0,2:T(2,128)(2,1)} all-to-all(bf16[2,256,8192]{1,0,2:T(2,128)(2,1)} %copy.21), channel_id=1, replica_groups=mesh['freq'=4,'row'=8] {'row'}, dimensions={2} | all-to-all | bytes 16777216 | tf_op jit(solution)/shard_map/all_to_all | solution.py:55
  218.6 30.5 %copy.22 = bf16[2,8,256,1024]{3,0,2,1:T(2,128)(2,1)} copy(bf16[2,8,256,1024]{2,0,3,1:T(2,128)(2,1)} %bitcast.66) | data formatting | bytes 16777216 | tf_op jit(solution)/shard_map/all_to_all | solution.py:55
  249.1 0.0 collective-permute-start
  249.1 13.5 collective-permute-done
  262.6 15.7 broadcast_select_fusion.5
  278.3 0.0 copy-start
  278.3 0.0 copy-start.1
  278.3 0.0 copy-start.3
  278.3 0.0 copy-start.4
  278.4 26.5 %pad_maximum_fusion.2 = bf16[2,2,2048,1024]{3,1,2,0:T(2,128)(2,1)} fusion(bf16[1,2,2048,1024]{3,1,2,0:T(2,128)(2,1)S(1)} %get-tuple-element.23, bf16[1,2,2048,1024]{3,1,2,0:T(2,128)(2,1)S(1)} %get-tuple-element.22), kind=kLoop, calls=%fused_computation.9 | loop fusion | flops 8388608 | bytes 33554432 | tf_op jit(solution)/shard_map/concatenate | solution.py:25
  304.9 0.0 copy-done
  304.9 0.0 copy-done.1
  304.9 1.7 collective-permute-start.1
  306.5 0.0 copy-done.3
  306.5 0.6 fusion.49
  311.9 0.0 copy-done.4
  311.9 0.1 cosine_convert_fusion
  312.0 0.2 fusion.45
  312.2 355.3 %collective-permute-done.1 = bf16[2,2,2048,1024]{3,1,2,0:T(2,128)(2,1)} collective-permute-done((bf16[2,2,2048,1024]{3,1,2,0:T(2,128)(2,1)}, bf16[2,2,2048,1024]{3,1,2,0:T(2,128)(2,1)}, u32[]{:S(2)}, u32[]{:S(2)}) %collective-permute-start.1) | collective-permute-done | bytes 16777248 | tf_op jit(solution)/shard_map/ppermute | solution.py:23
  667.5 43.1 %broadcast_select_fusion.1 = (bf16[2,2,2048,1024]{3,1,2,0:T(2,128)(2,1)S(1)}, bf16[2,2,2048,1024]{3,1,2,0:T(2,128)(2,1)}) fusion(bf16[2,2,2048,1024]{3,1,2,0:T(2,128)(2,1)} %collective-permute-done.1, pred[]{:T(512)S(6)} %eq.17, bf16[1,2,2048,1024]{3,1,2,0:T(2,128)(2,1)} %copy-done.1, bf16[1,2,2048,1024]{3,1,2,0:T(2,128)(2,1)} %copy-done), kind=kLoop, calls=%fused_computation.8 | loop fusion | flops 25165824 | bytes 67108864 | tf_op jit(solution)/shard_map/jit(_where)/select_n | solution.py:25
  710.6 47.6 %pad_maximum_fusion = bf16[4,2,2048,1024]{3,1,2,0:T(2,128)(2,1)} fusion(bf16[2,2,2048,1024]{3,1,2,0:T(2,128)(2,1)} %get-tuple-element.21, bf16[2,2,2048,1024]{3,1,2,0:T(2,128)(2,1)S(1)} %get-tuple-element.20), kind=kLoop, calls=%fused_computation.3 | loop fusion | flops 16777216 | bytes 67108864 | tf_op jit(solution)/shard_map/concatenate | solution.py:25
  758.2 145.3 %fusion = bf16[2,8192,1024]{2,0,1:T(2,128)(2,1)} fusion(bf16[1,2,8192,1024]{3,2,1,0:T(8,128)(2,1)} %param.5, bf16[2,8192,1024]{2,0,1:T(2,128)(2,1)} %bitcast.65, bf16[2,2]{1,0:T(2,128)(2,1)S(1)} %fusion.45), kind=kOutput, calls=%fused_computation.1 | convolution fusion | flops 150994944 | bytes 100663304 | tf_op jit(solution)/shard_map/tsb,ct->csb/dot_general | solution.py:57
  903.6 17.5 %broadcast_select_fusion.3 = (bf16[2,8192,256]{2,0,1:T(2,128)(2,1)}, bf16[2,8192,256]{2,0,1:T(2,128)(2,1)}) fusion(pred[]{:T(512)S(6)} %eq.19, bf16[2,8192,1024]{2,0,1:T(2,128)(2,1)} %fusion, s32[]{:T(128)S(6)} %select_n.101, s32[]{:T(128)S(6)} %select_n.107, pred[]{:T(512)S(6)} %eq.20), kind=kLoop, calls=%fused_computation.11 | loop fusion | flops 8388608 | bytes 33554440 | tf_op jit(solution)/shard_map/jit(_where)/select_n | solution.py:31
  921.1 0.0 all-reduce.3.cloned.1.call-update
  922.3 23.4 %copy.23 = bf16[1,2,8192,1024]{3,2,1,0:T(8,128)(2,1)} copy(bf16[1,2,8192,1024]{3,1,2,0:T(2,128)(2,1)} %bitcast.63) | data formatting | bytes 67108864
  945.7 6.3 constant_dynamic-slice_fusion.3
  952.1 478.7 %all-reduce.3.cloned.1.call-done = (bf16[2,8192,256]{2,0,1:T(2,128)(2,1)}, bf16[2,8192,256]{2,0,1:T(2,128)(2,1)}) async-done(((bf16[2,8192,256]{2,0,1:T(2,128)(2,1)}, bf16[2,8192,256]{2,0,1:T(2,128)(2,1)}), (bf16[2,8192,256]{2,0,1:T(2,128)(2,1)}, bf16[2,8192,256]{2,0,1:T(2,128)(2,1)})) %all-reduce.3.cloned.1.call-update) | async-done | bytes 16777232 | tf_op jit(solution)/shard_map/psum | solution.py:32
  1430.8 32.9 %fusion.47 = (bf16[1,8192,256]{2,0,1:T(2,128)(2,1)}, bf16[1,8192,256]{2,0,1:T(2,128)(2,1)}, bf16[1,8192,256]{2,0,1:T(2,128)(2,1)}, bf16[1,8192,256]{2,0,1:T(2,128)(2,1)}) fusion(bf16[2,8192,256]{2,0,1:T(2,128)(2,1)} %get-tuple-element.12, bf16[2,8192,256]{2,0,1:T(2,128)(2,1)} %get-tuple-element.13), kind=kLoop, calls=%fused_computation.73 | loop fusion | bytes 33554432 | tf_op jit(solution)/shard_map/slice | solution.py:41
  1463.7 0.0 copy-start.2
  1463.7 19.5 %fusion.11 = f32[1024,8192]{1,0:T(8,128)} fusion(bf16[1,8192,256]{2,0,1:T(2,128)(2,1)} %get-tuple-element.32, bf16[1,256,1024]{2,0,1:T(2,128)(2,1)} %get-tuple-element.17), kind=kOutput, calls=%fused_computation.24 | convolution fusion | flops 4294967296 | bytes 38273024 | tf_op jit(solution)/shard_map/dot_general | solution.py:39
  1483.1 0.0 copy-done.2
  1483.1 16.7 fusion.13
  1499.8 16.5 fusion.15
  1516.4 16.5 fusion.9
  1532.9 16.5 fusion.7
  1549.5 17.7 %fusion.3 = f32[1024,8192]{1,0:T(8,128)} fusion(bf16[1,8192,256]{2,0,1:T(2,128)(2,1)} %get-tuple-element.25, bf16[1,256,1024]{2,0,1:T(2,128)(2,1)S(1)} %get-tuple-element.15), kind=kOutput, calls=%fused_computation.16 | convolution fusion | flops 4294967296 | bytes 38273024 | tf_op jit(solution)/shard_map/dot_general | solution.py:39
  1567.1 40.7 %fusion.1 = bf16[1,1,1024,8192]{3,2,1,0:T(8,128)(2,1)} fusion(f32[1024,8192]{1,0:T(8,128)} %fusion.7, f32[1024,8192]{1,0:T(8,128)} %fusion.15, f32[1024,8192]{1,0:T(8,128)} %fusion.11, bf16[1,8192,256]{2,0,1:T(2,128)(2,1)} %get-tuple-element.25, bf16[1,256,1024]{2,0,1:T(2,128)(2,1)S(1)} %get-tuple-element.14), kind=kOutput, calls=%fused_computation.14 | convolution fusion | flops 4328521728 | bytes 122159104 | tf_op jit(solution)/shard_map/dot_general | solution.py:39
  1607.8 40.6 %fusion.2 = bf16[1,1,1024,8192]{3,2,1,0:T(8,128)(2,1)} fusion(f32[1024,8192]{1,0:T(8,128)} %fusion.3, f32[1024,8192]{1,0:T(8,128)} %fusion.9, f32[1024,8192]{1,0:T(8,128)} %fusion.13, bf16[1,8192,256]{2,0,1:T(2,128)(2,1)} %get-tuple-element.24, bf16[1,256,1024]{2,0,1:T(2,128)(2,1)S(1)} %get-tuple-element.14), kind=kOutput, calls=%fused_computation.15 | convolution fusion | flops 4328521728 | bytes 122159104 | tf_op jit(solution)/shard_map/dot_general | solution.py:39
  1648.5 23.0 %pad_maximum_fusion.1 = bf16[1,2,1024,8192]{3,2,1,0:T(8,128)(2,1)} fusion(bf16[1,1,1024,8192]{3,2,1,0:T(8,128)(2,1)} %fusion.2, bf16[1,1,1024,8192]{3,2,1,0:T(8,128)(2,1)} %fusion.1), kind=kLoop, calls=%fused_computation.4 | loop fusion | flops 16777216 | bytes 67108864 | tf_op jit(solution)/shard_map/stack | solution.py:74
  (1 shorter events, 0.0 us)
Async XLA Ops:
  7.2 1423.6 %all-reduce.3.cloned.1.call-start = ((), (), s32[]{:S(2)}) async-start(), calls=%async_computation.1 | async-start | bytes 33554432 | tf_op jit(solution)/shard_map/psum | solution.py:32
  249.1 13.5 collective-permute-start
  278.3 26.5 %copy-start = (bf16[1,2,2048,1024]{3,1,2,0:T(2,128)(2,1)}, bf16[1,2,2048,1024]{3,1,2,0:T(2,128)(2,1)S(1)}, u32[]{:S(2)}) copy-start(bf16[1,2,2048,1024]{3,1,2,0:T(2,128)(2,1)S(1)} %get-tuple-element.22) | copy-start | bytes 25165828
  278.3 26.5 %copy-start.1 = (bf16[1,2,2048,1024]{3,1,2,0:T(2,128)(2,1)}, bf16[1,2,2048,1024]{3,1,2,0:T(2,128)(2,1)S(1)}, u32[]{:S(2)}) copy-start(bf16[1,2,2048,1024]{3,1,2,0:T(2,128)(2,1)S(1)} %get-tuple-element.23) | copy-start | bytes 25165828
  278.3 28.2 %copy-start.3 = (s32[2]{0:T(128)S(1)}, s32[2]{0:T(128)}, u32[]{:S(2)}) copy-start(s32[2]{0:T(128)} %param.7) | copy-start | bytes 28
  278.3 33.6 %copy-start.4 = (s32[4]{0:T(128)S(1)}, s32[4]{0:T(128)}, u32[]{:S(2)}) copy-start(s32[4]{0:T(128)} %param.6) | copy-start | bytes 52
  304.9 362.6 %collective-permute-start.1 = (bf16[2,2,2048,1024]{3,1,2,0:T(2,128)(2,1)}, bf16[2,2,2048,1024]{3,1,2,0:T(2,128)(2,1)}, u32[]{:S(2)}, u32[]{:S(2)}) collective-permute-start(bf16[2,2,2048,1024]{3,1,2,0:T(2,128)(2,1)} %pad_maximum_fusion.2), channel_id=1, source_target_pairs={{0,16},{8,24},{16,0},{24,8},{1,17},{9,25},{17,1},{25,9},{2,18},{10... | collective-permute-start | bytes 50331656 | tf_op jit(solution)/shard_map/ppermute | solution.py:23
  1463.7 19.5 %copy-start.2 = (bf16[1,256,1024]{2,0,1:T(2,128)(2,1)S(1)}, bf16[1,256,1024]{2,0,1:T(2,128)(2,1)}, u32[]{:S(2)}) copy-start(bf16[1,256,1024]{2,0,1:T(2,128)(2,1)} %get-tuple-element.17) | copy-start | bytes 1572868
Sparse Core Ops, SparseCore 0:
  921.2 509.5 all-reduce.2
